TPU v7x, 256 devices: a whole 4x4x8 slice. The times are simulated.
256 devices in a mesh: obs: 4 (over y), blk: 64 (over x, z, core).
Axes of the slice: x: 4, y: 4, z: 8, core: 2. Of those that a mesh axis runs over, the one named last changes fastest.
Arguments:
- design_tiles: float32 [32768, 8, 128], P(('obs', 'blk')), may hold values from -8 to 8
- block_ids: int32 [32768, 8], P(('obs', 'blk')), may hold values from 0 to 63, as said below
- obs_weight: float32 [32768], P(('obs', 'blk')), may hold values from 4.8828126e-05 to 0.00048828125
- block_owner: int32 [64], replicated, may hold values from 0 to 63, each once
- prior_weight: float32 [512], replicated, may hold values from 0.25 to 1
Outputs:
- panel_factor: float32 [8192, 256], P('blk')
- panel_update: float32 [8192, 256], P('blk')
Inputs may be any that keep to these rules, and one draw needn't show every extreme that they name: `block_ids`: the 8 blocks of an observation are distinct. Among the 128 observations of one device (aligned blocks of rows) no block is named by more than 24 of them, and in every draw some device has a block named by exactly 24. `block_owner`: A permutation: each owner index once.
All inputs are finite; a program needn't handle non-finite values.
Results may differ from a plain program's by a relative error of at most 0.0003.
Values sent between devices are 32-bit elements; how exact they have to be, the bound alone decides.
No kernel may reach another device: no remote copies, remote signals or barrier semaphores. Data moves between devices by JAX's collectives and lax.ppermute only.
A program may use at most 64 MiB of HBM per device.

v0:
```python
import jax
import jax.numpy as jnp
from jax import lax
from jax.sharding import PartitionSpec as P


def back_solve(factor, right_rows):
    return jax.scipy.linalg.solve_triangular(factor, right_rows.T, lower=True).T


def with_prior(owned, row_index, prior_weight):
    col_index = jnp.arange(prior_weight.shape[0], dtype=jnp.int32)
    return owned + jnp.where(col_index[None, :] == row_index[:, None], prior_weight[None, :], 0.0)


def placed_square(owned, row_index, panel_cols):
    col_index = jnp.arange(panel_cols, dtype=jnp.int32)
    placing = (row_index[:, None] == col_index[None, :]).astype(jnp.float32)
    return jnp.einsum("rq,rp->qp", placing, owned, precision=lax.Precision.HIGHEST)


def finish_rows(owned, square, half_cols):
    mirrored = 0.5 * (square + square.T)
    factor = jnp.linalg.cholesky(mirrored[:half_cols, :half_cols])
    coupling = back_solve(factor, mirrored[half_cols:, :half_cols])
    first_rows = back_solve(factor, owned[:, :half_cols])
    update_rows = owned[:, half_cols:] - jnp.dot(
        first_rows, coupling.T, precision=lax.Precision.HIGHEST, preferred_element_type=jnp.float32
    )
    return (first_rows, update_rows)


def select_columns(labels, design_tiles, wanted):
    touched = design_tiles.shape[1]
    columns = jnp.zeros(
        (design_tiles.shape[0], wanted.shape[0], design_tiles.shape[2]), jnp.float32
    )
    for entry in range(touched):
        hit = labels[:, entry, None] == wanted[None, :]
        columns = columns + jnp.where(hit[:, :, None], design_tiles[:, entry, None, :], 0.0)
    return columns.reshape(design_tiles.shape[0], wanted.shape[0] * design_tiles.shape[2])


def local(design_tiles, block_ids, obs_weight, block_owner, prior_weight):
    block_width = design_tiles.shape[2]
    block_count = block_owner.shape[0]
    panel_cols = prior_weight.shape[0]
    half_cols = panel_cols // 2
    panel_blocks = panel_cols // block_width
    block_range = jnp.arange(block_count, dtype=jnp.int32)
    owner_index = lax.axis_index("blk")
    owner_block = jnp.sum(jnp.where(block_owner == owner_index, block_range, 0))
    slots = jnp.sum(
        jnp.where(
            block_ids[:, :, None] == block_range[None, None, :], block_owner[None, None, :], 0
        ),
        axis=2,
    )
    panel_design = select_columns(
        block_ids, design_tiles, jnp.arange(panel_blocks, dtype=jnp.int32)
    )
    weighted = panel_design * obs_weight[:, None]
    wanted = jnp.arange(lax.axis_size("blk") * block_width // block_width, dtype=jnp.int32)
    columns = select_columns(slots, design_tiles, wanted)
    partial_value = lax.psum_scatter(
        jnp.einsum("oi,op->ip", columns, weighted, precision=lax.Precision.HIGHEST),
        "blk",
        scatter_dimension=0,
        tiled=True,
    )
    owned = lax.psum(partial_value, "obs")
    row_index = owner_block * block_width + jnp.arange(block_width, dtype=jnp.int32)
    owned = with_prior(owned, row_index, prior_weight)
    square = lax.psum(placed_square(owned, row_index, panel_cols), "blk")
    first_rows, update_rows = finish_rows(owned, square, half_cols)
    return (first_rows, update_rows)


def solution(mesh):
    in_specs = (P(("obs", "blk"), None, None), P(("obs", "blk"), None), P(("obs", "blk")), P(), P())
    out_specs = (P("blk", None), P("blk", None))
    return jax.shard_map(local, mesh=mesh, in_specs=in_specs, out_specs=out_specs, check_vma=False)
```

profile of v0, /device:TPU:8, one launch (start us, length us, event | category | flops | bytes accessed | tf_op | source)
XLA Modules:
  0.0 547.7 jit_solution(13729939461648007592)
XLA Ops:
  7.2 0.0 copy-start.1
  7.2 0.0 reduce-scatter.2.cloned.1.call-start
  7.2 1.0 slice_bitcast_fusion.15
  8.2 0.8 select_reduce_fusion
  9.0 3.5 fusion.27
  12.5 0.1 iota_compare_fusion.14
  12.6 0.1 iota_compare_fusion.16
  12.8 0.1 iota_compare_fusion.18
  12.9 0.1 iota_compare_fusion.20
  13.0 0.1 iota_compare_fusion.6
  13.1 0.1 iota_compare_fusion.8
  13.2 0.1 iota_compare_fusion.10
  13.3 0.1 iota_compare_fusion.12
  13.4 9.0 %select_add_fusion = f32[128,64,128]{2,1,0:T(8,128)S(1)} fusion(f32[128,128]{1,0:T(8,128)S(1)} %bitcast.108, f32[128,128]{1,0:T(8,128)S(1)} %bitcast.110, f32[128,128]{1,0:T(8,128)S(1)} %bitcast.98, f32[128,128]{1,0:T(8,128)S(1)} %bitcast.100, f32[128,128]{1,0:T(8,128)S(1)} %bitcast.102, f32[128,128]{1,0:T(8,128)S(1)} %bitcast.104, ...), kind=kLoop, calls=%fused_computation.5 | loop fusion | flops 15728640 | bytes 4784128 | tf_op jit(solution)/shard_map/add | solution.py:40
  22.4 0.0 copy-done.1
  22.4 1.6 add_multiply_fusion
  23.9 18.2 %fusion = f32[8192,512]{1,0:T(8,128)} fusion(f32[16,8,64,128]{3,2,1,0:T(8,128)S(1)} %bitcast.94, f32[16,8,4,128]{3,2,1,0:T(4,128)S(1)} %bitcast.95), kind=kOutput, calls=%fused_computation.2 | convolution fusion | flops 6442450944 | bytes 21233664 | tf_op jit(solution)/shard_map/oi,op->ip/dot_general | solution.py:66
  42.1 0.0 copy-start.2
  42.1 0.0 copy-start
  42.1 0.0 reduce-scatter.2.cloned.1.call-update
  42.2 0.0 all-reduce.4.cloned.1.call-start
  42.2 192.8 %reduce-scatter.2.cloned.1.call-done = f32[128,512]{1,0:T(8,128)} async-done(((f32[8192,512]{1,0:T(8,128)}), f32[128,512]{1,0:T(8,128)}) %reduce-scatter.2.cloned.1.call-update) | async-done | bytes 262160 | tf_op jit(solution)/shard_map/reduce_scatter | solution.py:65
  235.0 0.0 all-reduce.4.cloned.1.call-update
  235.0 0.2 all-reduce.6.cloned.1.call-start
  235.3 0.0 copy-done.2
  235.3 0.6 fusion.24
  236.6 45.1 %all-reduce.4.cloned.1.call-done = f32[128,512]{1,0:T(8,128)} async-done(((f32[128,512]{1,0:T(8,128)}), f32[128,512]{1,0:T(8,128)}) %all-reduce.4.cloned.1.call-update) | async-done | bytes 262160 | tf_op jit(solution)/shard_map/psum | solution.py:71
  281.7 0.0 copy-done
  281.7 1.0 select_add_fusion.1
  282.8 1.7 fusion.10
  284.5 0.0 all-reduce.6.cloned.1.call-update
  284.5 189.4 %all-reduce.6.cloned.1.call-done = f32[512,512]{1,0:T(8,128)} async-done(((f32[512,512]{1,0:T(8,128)}), f32[512,512]{1,0:T(8,128)}) %all-reduce.6.cloned.1.call-update) | async-done | bytes 1048592 | tf_op jit(solution)/shard_map/psum | solution.py:74
  474.0 1.6 copy.11
  475.5 1.4 fusion.3
  477.0 0.1 copy.12
  477.2 11.7 %cholesky.50 = f32[128,128]{1,0:T(8,128)S(1)} custom-call(f32[128,128]{1,0:T(8,128)S(1)} %cholesky.118), custom_call_target="Cholesky" | custom-call | tf_op jit(solution)/shard_map/jit(cholesky)/cholesky | solution.py:24
  489.0 9.8 %custom-call.18 = f32[1,128,128]{1,2,0:T(8,128)S(1)} custom-call(f32[1,128,128]{2,1,0:T(8,128)S(1)} %get-tuple-element.37), custom_call_target="InvertDiagBlocksLowerTriangular" | custom-call | tf_op jit(solution)/shard_map/jit(cholesky)/cholesky | solution.py:24
  498.8 0.2 constant_dynamic-update-slice_fusion.1
  499.0 0.3 convolution_subtract_fusion.3
  499.3 11.7 %cholesky.105 = f32[128,128]{1,0:T(8,128)S(1)} custom-call(f32[128,128]{1,0:T(8,128)S(1)} %convolution_subtract_fusion.3), custom_call_target="Cholesky" | custom-call | tf_op jit(solution)/shard_map/jit(cholesky)/cholesky | solution.py:24
  511.0 0.7 compare_reduce_fusion
  511.7 0.6 compare_reduce_fusion.1
  513.7 0.1 triangular_solve.72
  513.8 4.1 while.1
  514.0 0.6 fusion.36
  514.5 1.4 bitcast_dynamic-update-slice_fusion.2
  515.9 0.6 fusion.36
  516.5 1.4 bitcast_dynamic-update-slice_fusion.2
  517.9 19.7 %custom-call.19 = f32[2,128,128]{1,2,0:T(8,128)S(1)} custom-call(f32[2,128,128]{2,1,0:T(8,128)S(1)} %get-tuple-element.9), custom_call_target="InvertDiagBlocksLowerTriangular" | custom-call | tf_op jit(solution)/shard_map/jit(_solve_triangular)/triangular_solve | solution.py:8
  537.6 0.3 fusion.11
  537.9 0.3 convolution_subtract_fusion.1
  538.2 0.3 fusion.20
  538.5 0.3 fusion.15
  538.8 0.3 convolution_subtract_fusion.2
  539.1 0.3 fusion.21
  539.4 1.1 convolution_subtract_fusion
  540.4 0.8 copy.13
  (15 shorter events, 0.3 us)
Async XLA Ops:
  7.2 15.2 %copy-start.1 = (f32[128]{0:T(128)S(1)}, f32[128]{0:T(128)}, u32[]{:S(2)}) copy-start(f32[128]{0:T(128)} %param.7) | copy-start | bytes 1540
  7.2 227.8 %reduce-scatter.2.cloned.1.call-start = ((), (), s32[]{:S(2)}) async-start(), calls=%async_computation.1 | async-start | bytes 17039360 | tf_op jit(solution)/shard_map/reduce_scatter | solution.py:65
  42.1 193.2 %copy-start.2 = (s32[64]{0:T(128)S(1)}, s32[64]{0:T(128)}, u32[]{:S(2)}) copy-start(s32[64]{0:T(128)} %param.8) | copy-start | bytes 772
  42.1 239.6 %copy-start = (f32[512]{0:T(512)S(1)}, f32[512]{0:T(512)}, u32[]{:S(2)}) copy-start(f32[512]{0:T(512)} %param.9) | copy-start | bytes 6148
  42.2 239.6 %all-reduce.4.cloned.1.call-start = ((), (), s32[]{:S(2)}) async-start(), calls=%async_computation.2 | async-start | bytes 524288 | tf_op jit(solution)/shard_map/psum | solution.py:71
  235.0 238.9 %all-reduce.6.cloned.1.call-start = ((), (), s32[]{:S(2)}) async-start(), calls=%async_computation.3 | async-start | bytes 2097152 | tf_op jit(solution)/shard_map/psum | solution.py:74
Sparse Core Ops, SparseCore 0:
  42.3 192.7 reduce-scatter.1
  237.3 44.3 all-reduce.3
  285.1 188.7 all-reduce.5
where the time goes:
time: 548 us
  waiting for transfers between devices  427 us (78%)
  other arithmetic  69.7 us (13%)
  matrix products  23.1 us (4%)
  between operations  16 us (3%)
  local copies, waits for them, and re-layouts  11 us (2%)
    reduce_scatter x1, waiting for transfers between devices, local(): lax.psum_scatter(jnp.einsum('oi,op->ip', columns, weighted, precision=lax...  193 us
    psum x1, waiting for transfers between devices, local(): square = lax.psum(placed_square(owned, row_index, panel_cols), 'blk')  189 us
    psum x1, waiting for transfers between devices, local(): owned = lax.psum(partial_value, 'obs')  45.1 us
    another operation x7, other arithmetic, finish_rows(): factor = jnp.linalg.cholesky(mirrored[:half_cols, :half_cols])  34.6 us
    another operation x3, other arithmetic, back_solve(): return jax.scipy.linalg.solve_triangular(factor, right_rows.T, lower=True).T  19.7 us
    dot_general x1, matrix products, local(): jnp.einsum('oi,op->ip', columns, weighted, precision=lax.Precision.HIGHEST)  18.2 us
  transfers between devices with their start and end apart: 3, of which 3 were waited for; matrix products, arithmetic and copies ran while one was open for 0% of the time, Pallas kernels for 0%

commit v1 on v0

--- a/solution.py
+++ b/solution.py
@@ -2,6 +2,18 @@
 import jax.numpy as jnp
 from jax import lax
 from jax.sharding import PartitionSpec as P
+
+
+def time_units(my_data):
+    across = "obs"
+    n_now = my_data
+    axis_len = jax.lax.axis_size(across)
+    for dev_i in [
+        [(k0, k0 ^ i) for k0 in range(axis_len)] for i in (1, 2, 4, 8, 16) if i < axis_len
+    ]:
+        z_new = jax.lax.ppermute(n_now, across, perm=dev_i)
+        n_now = n_now + z_new
+    return n_now
 
 
 def back_solve(factor, right_rows):
@@ -68,7 +80,7 @@
         scatter_dimension=0,
         tiled=True,
     )
-    owned = lax.psum(partial_value, "obs")
+    owned = time_units(partial_value)
     row_index = owner_block * block_width + jnp.arange(block_width, dtype=jnp.int32)
     owned = with_prior(owned, row_index, prior_weight)
     square = lax.psum(placed_square(owned, row_index, panel_cols), "blk")

time: 548 us -> 514 us (0.938)
  waiting for transfers between devices: 427 us -> 389 us
    psum x1 -> x0, waiting for transfers between devices: 45.1 us -> none  [local(): owned = lax.psum(partial_value, 'obs')]
    ppermute x0 -> x2, waiting for transfers between devices: none -> 9.13 us  [time_units(): z_new = jax.lax.ppermute(n_now, across, perm=dev_i)]
  transfers between devices with their start and end apart: 3 -> 4, of which waited for: 3 -> 4; matrix products, arithmetic and copies ran while one was open for 0% -> 0% of each run, Pallas kernels for 0% -> 0%
where the time goes in v1:
time: 514 us
  waiting for transfers between devices  389 us (76%)
  other arithmetic  69.7 us (14%)
  matrix products  23.1 us (4%)
  between operations  16.2 us (3%)
  local copies, waits for them, and re-layouts  11 us (2%)
    reduce_scatter x1, waiting for transfers between devices, local(): lax.psum_scatter(jnp.einsum('oi,op->ip', columns, weighted, precision=lax...  193 us
    psum x1, waiting for transfers between devices, local(): square = lax.psum(placed_square(owned, row_index, panel_cols), 'blk')  187 us
    another operation x7, other arithmetic, finish_rows(): factor = jnp.linalg.cholesky(mirrored[:half_cols, :half_cols])  34.6 us
    another operation x3, other arithmetic, back_solve(): return jax.scipy.linalg.solve_triangular(factor, right_rows.T, lower=True).T  19.7 us
    dot_general x1, matrix products, local(): jnp.einsum('oi,op->ip', columns, weighted, precision=lax.Precision.HIGHEST)  18.2 us
  transfers between devices with their start and end apart: 4, of which 4 were waited for; matrix products, arithmetic and copies ran while one was open for 0% of the time, Pallas kernels for 0%

profile of v1, /device:TPU:8, one launch (start us, length us, event | category | flops | bytes accessed | tf_op | source)
XLA Modules:
  0.0 513.9 jit_solution(6014039921650060898)
XLA Ops:
  7.2 0.0 copy-start.1
  7.2 0.0 reduce-scatter.2.cloned.1.call-start
  7.2 1.0 slice_bitcast_fusion.15
  8.2 0.8 select_reduce_fusion
  9.0 3.5 fusion.31
  12.5 0.1 iota_compare_fusion.14
  12.6 0.1 iota_compare_fusion.16
  12.8 0.1 iota_compare_fusion.18
  12.9 0.1 iota_compare_fusion.20
  13.0 0.1 iota_compare_fusion.6
  13.1 0.1 iota_compare_fusion.8
  13.2 0.1 iota_compare_fusion.10
  13.3 0.1 iota_compare_fusion.12
  13.4 9.0 %select_add_fusion = f32[128,64,128]{2,1,0:T(8,128)S(1)} fusion(f32[128,128]{1,0:T(8,128)S(1)} %bitcast.107, f32[128,128]{1,0:T(8,128)S(1)} %bitcast.109, f32[128,128]{1,0:T(8,128)S(1)} %bitcast.97, f32[128,128]{1,0:T(8,128)S(1)} %bitcast.99, f32[128,128]{1,0:T(8,128)S(1)} %bitcast.101, f32[128,128]{1,0:T(8,128)S(1)} %bitcast.103, ...), kind=kLoop, calls=%fused_computation.5 | loop fusion | flops 15728640 | bytes 4784128 | tf_op jit(solution)/shard_map/add | solution.py:52
  22.4 0.0 copy-done.1
  22.4 1.6 add_multiply_fusion
  23.9 18.2 %fusion = f32[8192,512]{1,0:T(8,128)} fusion(f32[16,8,64,128]{3,2,1,0:T(8,128)S(1)} %bitcast.93, f32[16,8,4,128]{3,2,1,0:T(4,128)S(1)} %bitcast.94), kind=kOutput, calls=%fused_computation.2 | convolution fusion | flops 6442450944 | bytes 21233664 | tf_op jit(solution)/shard_map/oi,op->ip/dot_general | solution.py:78
  42.1 0.0 copy-start.2
  42.1 0.0 copy-start
  42.1 0.0 reduce-scatter.2.cloned.1.call-update
  42.1 0.0 all-reduce.3.cloned.1.call-start
  42.2 192.7 %reduce-scatter.2.cloned.1.call-done = f32[128,512]{1,0:T(8,128)} async-done(((f32[8192,512]{1,0:T(8,128)}), f32[128,512]{1,0:T(8,128)}) %reduce-scatter.2.cloned.1.call-update) | async-done | bytes 262160 | tf_op jit(solution)/shard_map/reduce_scatter | solution.py:77
  234.9 0.5 collective-permute-start
  235.4 6.1 %collective-permute-done = f32[128,512]{1,0:T(8,128)S(1)} collective-permute-done((f32[128,512]{1,0:T(8,128)}, f32[128,512]{1,0:T(8,128)S(1)}, u32[]{:S(2)}, u32[]{:S(2)}) %collective-permute-start) | collective-permute-done | bytes 262176 | tf_op jit(solution)/shard_map/ppermute | solution.py:14
  241.5 1.0 add.225
  242.5 4.5 collective-permute-start.1
  247.0 0.0 copy-done.2
  247.0 0.6 fusion.28
  248.3 3.1 collective-permute-done.1
  251.3 0.0 copy-done
  251.3 0.1 select_add_fusion.1
  251.4 1.7 fusion.11
  253.1 0.0 all-reduce.3.cloned.1.call-update
  253.2 186.7 %all-reduce.3.cloned.1.call-done = f32[512,512]{1,0:T(8,128)} async-done(((f32[512,512]{1,0:T(8,128)}), f32[512,512]{1,0:T(8,128)}) %all-reduce.3.cloned.1.call-update) | async-done | bytes 1048592 | tf_op jit(solution)/shard_map/psum | solution.py:86
  439.9 1.6 copy.11
  441.5 1.4 fusion.3
  443.0 0.1 copy.12
  443.2 11.7 %cholesky.50 = f32[128,128]{1,0:T(8,128)S(1)} custom-call(f32[128,128]{1,0:T(8,128)S(1)} %cholesky.118), custom_call_target="Cholesky" | custom-call | tf_op jit(solution)/shard_map/jit(cholesky)/cholesky | solution.py:36
  455.0 9.8 %custom-call.18 = f32[1,128,128]{1,2,0:T(8,128)S(1)} custom-call(f32[1,128,128]{2,1,0:T(8,128)S(1)} %get-tuple-element.37), custom_call_target="InvertDiagBlocksLowerTriangular" | custom-call | tf_op jit(solution)/shard_map/jit(cholesky)/cholesky | solution.py:36
  464.8 0.2 constant_dynamic-update-slice_fusion.1
  465.0 0.3 convolution_subtract_fusion.1
  465.3 11.7 %cholesky.105 = f32[128,128]{1,0:T(8,128)S(1)} custom-call(f32[128,128]{1,0:T(8,128)S(1)} %convolution_subtract_fusion.1), custom_call_target="Cholesky" | custom-call | tf_op jit(solution)/shard_map/jit(cholesky)/cholesky | solution.py:36
  477.0 0.7 compare_reduce_fusion
  477.7 0.6 compare_reduce_fusion.1
  479.6 0.1 triangular_solve.72
  479.7 4.1 while.1
  479.9 0.6 fusion.39
  480.5 1.4 bitcast_dynamic-update-slice_fusion.2
  481.8 0.6 fusion.39
  482.4 1.4 bitcast_dynamic-update-slice_fusion.2
  483.8 19.7 %custom-call.19 = f32[2,128,128]{1,2,0:T(8,128)S(1)} custom-call(f32[2,128,128]{2,1,0:T(8,128)S(1)} %get-tuple-element.9), custom_call_target="InvertDiagBlocksLowerTriangular" | custom-call | tf_op jit(solution)/shard_map/jit(_solve_triangular)/triangular_solve | solution.py:20
  503.5 0.3 fusion.12
  503.8 0.3 convolution_subtract_fusion
  504.1 0.3 fusion.24
  504.4 0.3 fusion.19
  504.7 0.3 fusion.26
  505.0 0.3 fusion.18
  505.3 1.1 slice_subtract_fusion
  506.3 0.8 copy.13
  (15 shorter events, 0.3 us)
Async XLA Ops:
  7.2 15.2 %copy-start.1 = (f32[128]{0:T(128)S(1)}, f32[128]{0:T(128)}, u32[]{:S(2)}) copy-start(f32[128]{0:T(128)} %param.7) | copy-start | bytes 1540
  7.2 227.7 %reduce-scatter.2.cloned.1.call-start = ((), (), s32[]{:S(2)}) async-start(), calls=%async_computation.1 | async-start | bytes 17039360 | tf_op jit(solution)/shard_map/reduce_scatter | solution.py:77
  42.1 204.9 %copy-start.2 = (s32[64]{0:T(128)S(1)}, s32[64]{0:T(128)}, u32[]{:S(2)}) copy-start(s32[64]{0:T(128)} %param.8) | copy-start | bytes 772
  42.1 209.2 %copy-start = (f32[512]{0:T(512)S(1)}, f32[512]{0:T(512)}, u32[]{:S(2)}) copy-start(f32[512]{0:T(512)} %param.9) | copy-start | bytes 6148
  42.1 397.8 %all-reduce.3.cloned.1.call-start = ((), (), s32[]{:S(2)}) async-start(), calls=%async_computation.2 | async-start | bytes 2097152 | tf_op jit(solution)/shard_map/psum | solution.py:86
  234.9 6.6 %collective-permute-start = (f32[128,512]{1,0:T(8,128)}, f32[128,512]{1,0:T(8,128)S(1)}, u32[]{:S(2)}, u32[]{:S(2)}) collective-permute-start(f32[128,512]{1,0:T(8,128)} %reduce-scatter.2.cloned.1.call-done), channel_id=1, source_target_pairs={{0,64},{64,0},{128,192},{192,128},{1,65},{65,1},{129,193},{193,129... | collective-permute-start | bytes 786440 | tf_op jit(solution)/shard_map/ppermute | solution.py:14
  242.5 8.8 %collective-permute-start.1 = (f32[128,512]{1,0:T(8,128)S(1)}, f32[128,512]{1,0:T(8,128)S(1)}, u32[]{:S(2)}, u32[]{:S(2)}) collective-permute-start(f32[128,512]{1,0:T(8,128)S(1)} %add.225), channel_id=1, source_target_pairs={{0,128},{64,192},{128,0},{192,64},{1,129},{65,193},{129,1},{193,65... | collective-permute-start | bytes 786440 | tf_op jit(solution)/shard_map/ppermute | solution.py:14
Sparse Core Ops, SparseCore 0:
  42.3 192.5 reduce-scatter.1
  253.3 186.6 all-reduce.2
